TPU v7x, 512 devices: a whole 4x8x8 slice. The times are simulated.
512 devices in a mesh: dp: 4 (over x), shard: 128 (over z, y, core).
Axes of the slice: x: 4, y: 8, z: 8, core: 2. Of those that a mesh axis runs over, the one named last changes fastest.
Arguments:
- grad_parts: float32 [4, 1024, 16384], P('dp', None, 'shard'), may hold values from -0.3 to 0.3
- owner: int32 [1024], replicated, may hold values from 0 to 127, as said below
- master: float32 [4, 128, 4, 128, 128], P('dp', 'shard'), may hold values from -6 to 6
- first_moment: float32 [4, 128, 4, 128, 128], P('dp', 'shard'), may hold values from -0.12 to 0.12
- second_moment: float32 [4, 128, 4, 128, 128], P('dp', 'shard'), may hold values from 0.0001 to 0.001
- left_stat: float32 [4, 128, 4, 128, 128], P('dp', 'shard'), may hold values from -0.0062992126 to 10
- right_stat: float32 [4, 128, 4, 128, 128], P('dp', 'shard'), may hold values from -0.0062992126 to 10
- left_basis: float32 [4, 128, 4, 128, 128], P('dp', 'shard'), may hold values from -0.079549513 to 1.0795495
- right_basis: float32 [4, 128, 4, 128, 128], P('dp', 'shard'), may hold values from -0.079549513 to 1.0795495
Outputs:
- new_params: bfloat16 [1024, 16384], P(None, 'shard')
- master_out: float32 [4, 128, 4, 128, 128], P('dp', 'shard')
- first_out: float32 [4, 128, 4, 128, 128], P('dp', 'shard')
- second_out: float32 [4, 128, 4, 128, 128], P('dp', 'shard')
- left_stat_out: float32 [4, 128, 4, 128, 128], P('dp', 'shard')
- right_stat_out: float32 [4, 128, 4, 128, 128], P('dp', 'shard')
- left_basis_out: float32 [4, 128, 4, 128, 128], P('dp', 'shard')
- right_basis_out: float32 [4, 128, 4, 128, 128], P('dp', 'shard')
Inputs may be any that keep to these rules, and one draw needn't show every extreme that they name: In each group of 256 consecutive tiles no owner index holds more than 4 tiles, and some owner holds exactly 4.
All inputs are finite; a program needn't handle non-finite values.
Results may differ from a plain program's by a relative error of at most 0.001.
Values may be sent and summed in bfloat16 or wider, within the bound.
No kernel may reach another device: no remote copies, remote signals or barrier semaphores. Data moves between devices by JAX's collectives and lax.ppermute only.
A program may use at most 64 MiB of HBM per device.

v0:
```python
import jax
import jax.numpy as jnp
from jax import lax
from jax.sharding import PartitionSpec as P

NS_STEPS = 10
beta_one = 0.9
beta_two = 0.95
stat_decay = 0.95
learn_rate = 0.05
weight_decay = 0.01
adam_eps = 1e-08
highest = lax.Precision.HIGHEST


def product(form, left, right):
    return jnp.einsum(form, left, right, precision=highest)


def slot_index(owners, shards):
    matches = (owners[..., None] == jnp.arange(shards, dtype=jnp.int32)).astype(jnp.int32)
    running = jnp.cumsum(matches, axis=1)
    return jnp.sum(matches * running, axis=-1) - 1


def orthogonal(pending):
    iterate = pending * lax.rsqrt(jnp.sum(pending * pending, axis=(1, 2), keepdims=True) + 1e-06)
    for step in range(NS_STEPS):
        gram = product("nik,njk->nij", iterate, iterate)
        iterate = 1.5 * iterate - 0.5 * product("nij,njk->nik", gram, iterate)
    return iterate


def soap_update(gradient, master, first, second, lstat, rstat, lbasis, rbasis):
    first_new = beta_one * first + (1.0 - beta_one) * gradient
    grad_rot = product("nik,nkl->nil", product("nji,njk->nik", lbasis, gradient), rbasis)
    first_rot = product("nik,nkl->nil", product("nji,njk->nik", lbasis, first_new), rbasis)
    second_new = beta_two * second + (1.0 - beta_two) * grad_rot * grad_rot
    normed = first_rot / (jnp.sqrt(second_new) + adam_eps)
    update = product("nik,nlk->nil", product("nij,njk->nik", lbasis, normed), rbasis)
    master_new = master - learn_rate * (update + weight_decay * master)
    lstat_new = stat_decay * lstat + (1.0 - stat_decay) * product(
        "nik,njk->nij", gradient, gradient
    )
    rstat_new = stat_decay * rstat + (1.0 - stat_decay) * product(
        "nki,nkj->nij", gradient, gradient
    )
    lbasis_new = orthogonal(product("nij,njk->nik", lstat_new, lbasis))
    rbasis_new = orthogonal(product("nij,njk->nik", rstat_new, rbasis))
    return (master_new, first_new, second_new, lstat_new, rstat_new, lbasis_new, rbasis_new)


def body(
    grad_parts,
    owner,
    master,
    first_moment,
    second_moment,
    left_stat,
    right_stat,
    left_basis,
    right_basis,
):
    shards = lax.axis_size("shard")
    groups = lax.axis_size("dp")
    my_group = lax.axis_index("dp")
    capacity = master.shape[2]
    block_size = master.shape[4]
    piece_len = grad_parts.shape[2]
    tile_count = owner.shape[0]
    per_group = tile_count // groups
    owners = owner.reshape(groups, per_group)
    place_index = slot_index(owners, shards) * shards + owners
    own_place = lax.dynamic_index_in_dim(place_index, my_group, 0, keepdims=False)
    summed = lax.psum_scatter(grad_parts, "dp", scatter_dimension=1, tiled=True)
    outgoing = jnp.zeros((capacity * shards, piece_len), jnp.float32)
    outgoing = outgoing.at[own_place].set(summed[0])
    outgoing = outgoing.reshape(capacity, shards, piece_len)
    incoming = lax.all_to_all(outgoing, "shard", split_axis=1, concat_axis=1, tiled=True)

    def as_tiles(array):
        return array.reshape(capacity, block_size, block_size)

    results = soap_update(
        incoming,
        as_tiles(master),
        as_tiles(first_moment),
        as_tiles(second_moment),
        as_tiles(left_stat),
        as_tiles(right_stat),
        as_tiles(left_basis),
        as_tiles(right_basis),
    )
    shaped = [item.reshape(1, 1, capacity, block_size, block_size) for item in results]
    weights = results[0].astype(jnp.bfloat16)
    returned = lax.all_to_all(weights, "shard", split_axis=1, concat_axis=1, tiled=True)
    returned = returned.reshape(capacity * shards, piece_len)
    own_rows = returned[own_place]
    new_params = lax.all_gather(own_rows, "dp", axis=0, tiled=True)
    return (new_params, shaped[0], shaped[1], shaped[2], shaped[3], shaped[4], shaped[5], shaped[6])


def solution(mesh):
    placed = (
        P("dp", None, "shard"),
        P(),
        P("dp", "shard", None, None, None),
        P("dp", "shard", None, None, None),
        P("dp", "shard", None, None, None),
        P("dp", "shard", None, None, None),
        P("dp", "shard", None, None, None),
        P("dp", "shard", None, None, None),
        P("dp", "shard", None, None, None),
    )
    return jax.shard_map(
        body,
        mesh=mesh,
        in_specs=placed,
        out_specs=(
            P(None, "shard"),
            P("dp", "shard", None, None, None),
            P("dp", "shard", None, None, None),
            P("dp", "shard", None, None, None),
            P("dp", "shard", None, None, None),
            P("dp", "shard", None, None, None),
            P("dp", "shard", None, None, None),
            P("dp", "shard", None, None, None),
        ),
        check_vma=False,
    )
```

profile of v0, /device:TPU:8, one launch (start us, length us, event | category | flops | bytes accessed | tf_op | source)
XLA Modules:
  0.0 143.0 jit_solution(8679170944378737934)
XLA Ops:
  7.2 0.7 reduce-scatter.2.cloned.1.call-update
  7.9 0.7 copy-done.10
  8.8 0.9 fusion.26
  10.3 31.9 %reduce-scatter.2.cloned.1.call-done = f32[1,256,128]{2,1,0:T(8,128)} async-done(((f32[1,1024,128]{2,1,0:T(8,128)}), f32[1,256,128]{2,1,0:T(8,128)}) %reduce-scatter.2.cloned.1.call-update) | async-done | bytes 131088 | tf_op jit(solution)/shard_map/reduce_scatter | solution.py:75
  42.2 1.6 %scatter_custom_fusion = f32[512,128]{1,0:T(8,128)S(1)} fusion(s32[256]{0:T(256)S(1)} %bitcast.159, f32[1,256,128]{2,1,0:T(8,128)} %reduce-scatter.2.cloned.1.call-done, f32[]{:T(128)} %constant.18.clone.1), kind=kCustom, calls=%fused_computation.91 | custom fusion | bytes 393220 | tf_op jit(solution)/shard_map/scatter | solution.py:77
  43.8 0.9 copy.40
  44.7 14.5 %all-to-all-start = ((f32[4,128,128]{2,0,1:T(4,128)}), f32[4,128,128]{2,0,1:T(4,128)S(1)}, u32[]{:S(2)}, u32[]{:S(2)}) async-start(f32[4,128,128]{2,0,1:T(4,128)} %copy.40), calls=%async_computation.1 | async-start | bytes 524288 | tf_op jit(solution)/shard_map/all_to_all | solution.py:79
  59.2 14.5 %all-to-all-done = f32[4,128,128]{2,0,1:T(4,128)S(1)} async-done(((f32[4,128,128]{2,0,1:T(4,128)}), f32[4,128,128]{2,0,1:T(4,128)S(1)}, u32[]{:S(2)}, u32[]{:S(2)}) %all-to-all-start) | async-done | bytes 262176 | tf_op jit(solution)/shard_map/all_to_all | solution.py:79
  74.2 0.5 multiply_reduce_fusion
  74.9 0.8 fusion.51
  75.7 0.4 fusion.10
  76.1 0.7 fusion.76
  76.8 0.4 fusion.9
  77.2 0.7 fusion.77
  77.9 0.4 fusion.8
  78.3 0.7 fusion.78
  78.9 0.4 fusion.7
  79.4 0.7 fusion.79
  80.0 0.4 fusion.6
  80.4 0.7 fusion.80
  81.1 0.4 fusion.5
  81.5 0.7 fusion.81
  82.2 0.4 fusion.4
  82.6 0.7 fusion.82
  83.3 0.4 fusion.3
  83.7 0.7 fusion.83
  84.3 0.4 fusion.2
  84.8 0.7 fusion.84
  85.7 0.6 fusion.43
  86.7 0.7 fusion.23
  87.3 0.5 multiply_reduce_fusion.1
  88.0 0.8 fusion.54
  88.8 0.4 fusion.21
  89.2 0.7 fusion.67
  89.9 0.4 fusion.20
  90.3 0.8 fusion.68
  91.2 0.4 fusion.19
  91.6 0.7 fusion.69
  92.3 0.4 fusion.18
  92.7 0.7 fusion.70
  93.3 0.4 fusion.17
  93.8 0.7 fusion.71
  94.4 0.4 fusion.16
  94.8 0.7 fusion.72
  95.5 0.4 fusion.15
  95.9 0.7 fusion.73
  96.6 0.4 fusion.14
  97.0 0.7 fusion.74
  97.7 0.4 fusion.13
  98.1 0.7 fusion.75
  99.0 0.6 fusion.45
  99.9 0.4 fusion.29
  100.4 0.4 convolution_divide_fusion
  101.4 0.6 copy-done.9
  102.0 1.4 fusion.66
  103.4 0.8 copy.47
  104.1 6.1 %all-to-all-start.1 = ((bf16[4,128,128]{2,0,1:T(4,128)(2,1)}), bf16[4,128,128]{2,0,1:T(4,128)(2,1)S(1)}, u32[]{:S(2)}, u32[]{:S(2)}) async-start(bf16[4,128,128]{2,0,1:T(4,128)(2,1)} %copy.47), calls=%async_computation.2 | async-start | bytes 262144 | tf_op jit(solution)/shard_map/all_to_all | solution.py:96
  110.2 0.7 copy.53
  111.0 1.1 fusion.1
  112.1 1.1 fusion.12
  113.2 9.1 %all-to-all-done.1 = bf16[4,128,128]{2,0,1:T(4,128)(2,1)S(1)} async-done(((bf16[4,128,128]{2,0,1:T(4,128)(2,1)}), bf16[4,128,128]{2,0,1:T(4,128)(2,1)S(1)}, u32[]{:S(2)}, u32[]{:S(2)}) %all-to-all-start.1) | async-done | bytes 131104 | tf_op jit(solution)/shard_map/all_to_all | solution.py:96
  122.3 0.9 gather_fusion
  123.2 12.3 %all-gather = bf16[1024,128]{1,0:T(8,128)(2,1)S(1)} all-gather(bf16[256,128]{1,0:T(8,128)(2,1)S(1)} %gather_fusion), channel_id=2, replica_groups=mesh['dp'=4,'shard'=128] {'dp'}, dimensions={0}, use_global_device_ids=true | all-gather | bytes 327680 | tf_op jit(solution)/shard_map/all_gather | solution.py:99
  135.5 0.7 copy.69
  (39 shorter events, 3.7 us)
Async XLA Ops:
  7.2 67.0 %copy-start = (f32[1,1,4,128,128]{4,3,2,1,0:T(8,128)S(1)}, f32[1,1,4,128,128]{4,3,2,1,0:T(8,128)}, u32[]{:S(2)}) copy-start(f32[1,1,4,128,128]{4,3,2,1,0:T(8,128)} %param.17) | copy-start | bytes 786436
  7.2 35.0 %reduce-scatter.2.cloned.1.call-start = ((), (), s32[]{:S(2)}) async-start(), calls=%async_computation.3 | async-start | bytes 655360 | tf_op jit(solution)/shard_map/reduce_scatter | solution.py:75
  7.9 0.7 copy-start.10
  44.6 14.5 %copy-start.6 = (f32[1,1,4,128,128]{4,3,2,1,0:T(8,128)S(1)}, f32[1,1,4,128,128]{4,3,2,1,0:T(8,128)}, u32[]{:S(2)}) copy-start(f32[1,1,4,128,128]{4,3,2,1,0:T(8,128)} %param.12) | copy-start | bytes 786436
  44.7 29.0 %all-to-all-start = ((f32[4,128,128]{2,0,1:T(4,128)}), f32[4,128,128]{2,0,1:T(4,128)S(1)}, u32[]{:S(2)}, u32[]{:S(2)}) async-start(f32[4,128,128]{2,0,1:T(4,128)} %copy.40), calls=%async_computation.1 | async-start | bytes 524288 | tf_op jit(solution)/shard_map/all_to_all | solution.py:79
  59.2 14.6 %copy-start.7 = (f32[1,1,4,128,128]{4,3,2,1,0:T(8,128)S(1)}, f32[1,1,4,128,128]{4,3,2,1,0:T(8,128)}, u32[]{:S(2)}) copy-start(f32[1,1,4,128,128]{4,3,2,1,0:T(8,128)} %param.15) | copy-start | bytes 786436
  74.2 0.7 copy-start.3
  84.8 1.0 copy-start.1
  85.7 0.9 copy-start.5
  87.3 0.7 copy-start.2
  99.0 1.0 copy-start.8
  100.3 0.7 copy-start.4
  101.1 0.9 copy-start.9
  104.1 18.2 %all-to-all-start.1 = ((bf16[4,128,128]{2,0,1:T(4,128)(2,1)}), bf16[4,128,128]{2,0,1:T(4,128)(2,1)S(1)}, u32[]{:S(2)}, u32[]{:S(2)}) async-start(bf16[4,128,128]{2,0,1:T(4,128)(2,1)} %copy.47), calls=%async_computation.2 | async-start | bytes 262144 | tf_op jit(solution)/shard_map/all_to_all | solution.py:96
Sparse Core Ops, SparseCore 0:
  10.8 31.2 reduce-scatter.1
where the time goes:
time: 143 us
  waiting for transfers between devices  56.1 us (39%)
  matrix products  28.9 us (20%)
  starting transfers between devices  20.6 us (14%)
  between operations  14.6 us (10%)
  blocking collectives  12.3 us (9%)
  local copies, waits for them, and re-layouts  8.78 us (6%)
  other arithmetic  1.75 us (1%)
    reduce_scatter x1, waiting for transfers between devices, body(): summed = lax.psum_scatter(grad_parts, 'dp', scatter_dimension=1, tiled=True)  31.9 us
    dot_general x50, matrix products, product(): return jnp.einsum(form, left, right, precision=highest)  28.9 us
    all_to_all x1, waiting for transfers between devices, body(): lax.all_to_all(outgoing, 'shard', split_axis=1, concat_axis=1, tiled=True)  14.5 us
    all_to_all x1, starting transfers between devices, body(): lax.all_to_all(outgoing, 'shard', split_axis=1, concat_axis=1, tiled=True)  14.5 us
    all_gather x1, blocking collectives, body(): new_params = lax.all_gather(own_rows, 'dp', axis=0, tiled=True)  12.3 us
    all_to_all x1, waiting for transfers between devices, body(): lax.all_to_all(weights, 'shard', split_axis=1, concat_axis=1, tiled=True)  9.13 us
    all_to_all x1, starting transfers between devices, body(): lax.all_to_all(weights, 'shard', split_axis=1, concat_axis=1, tiled=True)  6.1 us
    unnamed x24, local copies, waits for them, and re-layouts  4.36 us
  transfers between devices with their start and end apart: 3, of which 3 were waited for; matrix products, arithmetic and copies ran while one was open for 3% of the time, Pallas kernels for 0%

commit v1 on v0

--- a/solution.py
+++ b/solution.py
@@ -96,7 +96,16 @@
     returned = lax.all_to_all(weights, "shard", split_axis=1, concat_axis=1, tiled=True)
     returned = returned.reshape(capacity * shards, piece_len)
     own_rows = returned[own_place]
-    new_params = lax.all_gather(own_rows, "dp", axis=0, tiled=True)
+    ways = lax.axis_size("dp")
+    up = [(d, (d + 1) % ways) for d in range(ways)]
+    down = [(d, (d - 1) % ways) for d in range(ways)]
+    earlier, later = ([own_rows], [own_rows])
+    for _ in range(ways // 2):
+        earlier.append(lax.ppermute(earlier[-1], "dp", up))
+    for _ in range((ways - 1) // 2):
+        later.append(lax.ppermute(later[-1], "dp", down))
+    line = jnp.concatenate([*earlier[::-1], *later[1:]], axis=0)
+    new_params = jnp.roll(line, (lax.axis_index("dp") - ways // 2) * own_rows.shape[0], axis=0)
     return (new_params, shaped[0], shaped[1], shaped[2], shaped[3], shaped[4], shaped[5], shaped[6])
 
 

time: 143 us -> 139 us (0.972)
  the two profiles are of different devices: /device:TPU:8 before, /device:TPU:6 now
where the time goes in v1:
time: 139 us; the launch traced here: 138 us
  waiting for transfers between devices  52.5 us (38%)
  starting transfers between devices  32.3 us (23%)
  matrix products  28.9 us (21%)
  between operations  14.7 us (11%)
  local copies, waits for them, and re-layouts  7.92 us (6%)
  other arithmetic  1.74 us (1%)
    reduce_scatter x1, waiting for transfers between devices, body(): summed = lax.psum_scatter(grad_parts, 'dp', scatter_dimension=1, tiled=True)  31.1 us
    dot_general x50, matrix products, product(): return jnp.einsum(form, left, right, precision=highest)  28.9 us
    all_to_all x1, waiting for transfers between devices, body(): lax.all_to_all(outgoing, 'shard', split_axis=1, concat_axis=1, tiled=True)  14.6 us
    all_to_all x1, starting transfers between devices, body(): lax.all_to_all(outgoing, 'shard', split_axis=1, concat_axis=1, tiled=True)  14.1 us
    ppermute x2, starting transfers between devices, body(): earlier.append(lax.ppermute(earlier[-1], 'dp', up))  9.94 us
    all_to_all x1, starting transfers between devices, body(): lax.all_to_all(weights, 'shard', split_axis=1, concat_axis=1, tiled=True)  6.35 us
    ppermute x1, waiting for transfers between devices, body(): later.append(lax.ppermute(later[-1], 'dp', down))  5.38 us
  transfers between devices with their start and end apart: 6, of which 4 were waited for; matrix products, arithmetic and copies ran while one was open for 20% of the time, Pallas kernels for 0%

profile of v1, /device:TPU:6, one launch (start us, length us, event | category | flops | bytes accessed | tf_op | source)
XLA Modules:
  0.0 138.1 jit_solution(15841297133683559648)
XLA Ops:
  7.2 0.7 reduce-scatter.2.cloned.1.call-update
  8.1 0.9 fusion.26
  9.7 31.1 %reduce-scatter.2.cloned.1.call-done = f32[1,256,128]{2,1,0:T(8,128)} async-done(((f32[1,1024,128]{2,1,0:T(8,128)}), f32[1,256,128]{2,1,0:T(8,128)}) %reduce-scatter.2.cloned.1.call-update) | async-done | bytes 131088 | tf_op jit(solution)/shard_map/reduce_scatter | solution.py:75
  40.7 1.6 %scatter_custom_fusion = f32[512,128]{1,0:T(8,128)S(1)} fusion(s32[256]{0:T(256)S(1)} %bitcast.159, f32[1,256,128]{2,1,0:T(8,128)} %reduce-scatter.2.cloned.1.call-done, f32[]{:T(128)} %constant.26.clone.1), kind=kCustom, calls=%fused_computation.91 | custom fusion | bytes 393220 | tf_op jit(solution)/shard_map/scatter | solution.py:77
  42.3 0.9 copy.40
  43.2 14.1 %all-to-all-start = ((f32[4,128,128]{2,0,1:T(4,128)}), f32[4,128,128]{2,0,1:T(4,128)S(1)}, u32[]{:S(2)}, u32[]{:S(2)}) async-start(f32[4,128,128]{2,0,1:T(4,128)} %copy.40), calls=%async_computation.1 | async-start | bytes 524288 | tf_op jit(solution)/shard_map/all_to_all | solution.py:79
  57.4 14.6 %all-to-all-done = f32[4,128,128]{2,0,1:T(4,128)S(1)} async-done(((f32[4,128,128]{2,0,1:T(4,128)}), f32[4,128,128]{2,0,1:T(4,128)S(1)}, u32[]{:S(2)}, u32[]{:S(2)}) %all-to-all-start) | async-done | bytes 262176 | tf_op jit(solution)/shard_map/all_to_all | solution.py:79
  72.3 0.6 fusion.45
  73.0 0.6 fusion.43
  73.9 0.4 fusion.29
  74.4 0.4 convolution_divide_fusion
  75.5 0.6 copy-done.8
  76.0 1.4 %fusion.66 = (bf16[4,128,128]{2,1,0:T(8,128)(2,1)S(1)}, f32[4,128,128]{2,1,0:T(8,128)}) fusion(f32[4,128,128]{1,2,0:T(8,128)S(1)} %fusion.41, f32[1,1,4,128,128]{4,3,2,1,0:T(8,128)S(1)} %copy-done, f32[1,1,4,128,128]{4,3,2,1,0:T(8,128)S(1)} %copy-done.8), kind=kOutput, calls=%fused_computation.116 | convolution fusion | flops 100990976 | bytes 1179648 | tf_op jit(solution)/shard_map/nik,nlk->nil/dot_general | solution.py:17
  77.4 0.8 copy.47
  78.2 6.4 %all-to-all-start.1 = ((bf16[4,128,128]{2,0,1:T(4,128)(2,1)}), bf16[4,128,128]{2,0,1:T(4,128)(2,1)S(1)}, u32[]{:S(2)}, u32[]{:S(2)}) async-start(bf16[4,128,128]{2,0,1:T(4,128)(2,1)} %copy.47), calls=%async_computation.2 | async-start | bytes 262144 | tf_op jit(solution)/shard_map/all_to_all | solution.py:96
  84.5 0.7 fusion.23
  85.2 0.5 multiply_reduce_fusion.1
  85.9 0.8 fusion.54
  86.7 0.4 fusion.21
  87.1 0.7 fusion.67
  87.8 0.4 fusion.20
  88.2 0.7 fusion.68
  88.9 0.4 fusion.19
  89.3 0.7 fusion.69
  89.9 0.4 fusion.18
  90.4 0.7 fusion.70
  91.0 0.4 fusion.17
  91.4 0.7 fusion.71
  92.1 0.4 fusion.16
  92.5 0.7 fusion.72
  93.2 0.4 fusion.15
  93.6 0.7 fusion.73
  94.3 0.4 fusion.14
  94.7 0.7 fusion.74
  95.3 0.4 fusion.13
  95.8 0.7 fusion.75
  97.1 0.5 multiply_reduce_fusion
  97.8 0.8 fusion.51
  98.6 0.4 fusion.10
  99.0 0.7 fusion.76
  99.7 0.4 fusion.9
  100.1 0.7 fusion.77
  100.8 0.4 fusion.8
  101.2 0.9 fusion.78
  102.1 0.4 fusion.7
  102.5 0.7 fusion.79
  103.6 0.7 fusion.80
  104.2 0.4 fusion.5
  104.6 0.7 fusion.81
  105.7 0.7 fusion.82
  106.4 0.4 fusion.3
  106.8 0.7 fusion.83
  107.5 0.4 fusion.2
  107.9 0.7 fusion.84
  108.6 0.9 gather_fusion
  109.4 4.5 %collective-permute-start = (bf16[256,128]{1,0:T(8,128)(2,1)S(1)}, bf16[256,128]{1,0:T(8,128)(2,1)S(1)}, u32[]{:S(2)}, u32[]{:S(2)}) collective-permute-start(bf16[256,128]{1,0:T(8,128)(2,1)S(1)} %gather_fusion), channel_id=1, source_target_pairs={{0,128},{128,256},{256,384},{384,0},{1,129},{129,257},{257,385},{3... | collective-permute-start | bytes 196616 | tf_op jit(solution)/shard_map/ppermute | solution.py:104
  113.9 1.1 fusion.12
  115.0 0.8 collective-permute-done
  115.8 5.5 %collective-permute-start.1 = (bf16[256,128]{1,0:T(8,128)(2,1)S(1)}, bf16[256,128]{1,0:T(8,128)(2,1)S(1)}, u32[]{:S(2)}, u32[]{:S(2)}) collective-permute-start(bf16[256,128]{1,0:T(8,128)(2,1)S(1)} %collective-permute-done), channel_id=1, source_target_pairs={{0,128},{128,256},{256,384},{384,0},{1,129},{129,257},{257,385},{3... | collective-permute-start | bytes 196616 | tf_op jit(solution)/shard_map/ppermute | solution.py:104
  121.3 1.1 fusion.1
  122.4 0.7 copy.53
  123.1 1.9 %collective-permute-start.2 = (bf16[256,128]{1,0:T(8,128)(2,1)S(1)}, bf16[256,128]{1,0:T(8,128)(2,1)S(1)}, u32[]{:S(2)}, u32[]{:S(2)}) collective-permute-start(bf16[256,128]{1,0:T(8,128)(2,1)S(1)} %gather_fusion), channel_id=1, source_target_pairs={{0,384},{128,0},{256,128},{384,256},{1,385},{129,1},{257,129},{385... | collective-permute-start | bytes 196616 | tf_op jit(solution)/shard_map/ppermute | solution.py:106
  125.1 5.4 %collective-permute-done.2 = bf16[256,128]{1,0:T(8,128)(2,1)S(1)} collective-permute-done((bf16[256,128]{1,0:T(8,128)(2,1)S(1)}, bf16[256,128]{1,0:T(8,128)(2,1)S(1)}, u32[]{:S(2)}, u32[]{:S(2)}) %collective-permute-start.2) | collective-permute-done | bytes 65568 | tf_op jit(solution)/shard_map/ppermute | solution.py:106
  130.5 0.7 constant_dynamic-slice_fusion
  (52 shorter events, 4.3 us)
Async XLA Ops:
  7.2 66.4 %copy-start = (f32[1,1,4,128,128]{4,3,2,1,0:T(8,128)S(1)}, f32[1,1,4,128,128]{4,3,2,1,0:T(8,128)}, u32[]{:S(2)}) copy-start(f32[1,1,4,128,128]{4,3,2,1,0:T(8,128)} %param.17) | copy-start | bytes 786436
  7.2 33.5 %reduce-scatter.2.cloned.1.call-start = ((), (), s32[]{:S(2)}) async-start(), calls=%async_computation.3 | async-start | bytes 655360 | tf_op jit(solution)/shard_map/reduce_scatter | solution.py:75
  7.2 0.7 copy-start.10
  43.2 14.1 %copy-start.6 = (f32[1,1,4,128,128]{4,3,2,1,0:T(8,128)S(1)}, f32[1,1,4,128,128]{4,3,2,1,0:T(8,128)}, u32[]{:S(2)}) copy-start(f32[1,1,4,128,128]{4,3,2,1,0:T(8,128)} %param.12) | copy-start | bytes 786436
  43.2 28.8 %all-to-all-start = ((f32[4,128,128]{2,0,1:T(4,128)}), f32[4,128,128]{2,0,1:T(4,128)S(1)}, u32[]{:S(2)}, u32[]{:S(2)}) async-start(f32[4,128,128]{2,0,1:T(4,128)} %copy.40), calls=%async_computation.1 | async-start | bytes 524288 | tf_op jit(solution)/shard_map/all_to_all | solution.py:79
  57.4 14.9 %copy-start.1 = (f32[1,1,4,128,128]{4,3,2,1,0:T(8,128)S(1)}, f32[1,1,4,128,128]{4,3,2,1,0:T(8,128)}, u32[]{:S(2)}) copy-start(f32[1,1,4,128,128]{4,3,2,1,0:T(8,128)} %param.16) | copy-start | bytes 786436
  73.0 1.0 copy-start.7
  74.4 0.7 copy-start.3
  75.1 0.9 copy-start.8
  77.4 7.1 %copy-start.5 = (f32[1,1,4,128,128]{4,3,2,1,0:T(8,128)S(1)}, f32[1,1,4,128,128]{4,3,2,1,0:T(8,128)}, u32[]{:S(2)}) copy-start(f32[1,1,4,128,128]{4,3,2,1,0:T(8,128)} %param.14) | copy-start | bytes 786436
  78.2 30.4 %all-to-all-start.1 = ((bf16[4,128,128]{2,0,1:T(4,128)(2,1)}), bf16[4,128,128]{2,0,1:T(4,128)(2,1)S(1)}, u32[]{:S(2)}, u32[]{:S(2)}) async-start(bf16[4,128,128]{2,0,1:T(4,128)(2,1)} %copy.47), calls=%async_computation.2 | async-start | bytes 262144 | tf_op jit(solution)/shard_map/all_to_all | solution.py:96
  85.2 0.7 copy-start.2
  95.8 1.0 copy-start.9
  97.1 0.7 copy-start.4
  109.4 6.4 %collective-permute-start = (bf16[256,128]{1,0:T(8,128)(2,1)S(1)}, bf16[256,128]{1,0:T(8,128)(2,1)S(1)}, u32[]{:S(2)}, u32[]{:S(2)}) collective-permute-start(bf16[256,128]{1,0:T(8,128)(2,1)S(1)} %gather_fusion), channel_id=1, source_target_pairs={{0,128},{128,256},{256,384},{384,0},{1,129},{129,257},{257,385},{3... | collective-permute-start | bytes 196616 | tf_op jit(solution)/shard_map/ppermute | solution.py:104
  115.8 9.2 %collective-permute-start.1 = (bf16[256,128]{1,0:T(8,128)(2,1)S(1)}, bf16[256,128]{1,0:T(8,128)(2,1)S(1)}, u32[]{:S(2)}, u32[]{:S(2)}) collective-permute-start(bf16[256,128]{1,0:T(8,128)(2,1)S(1)} %collective-permute-done), channel_id=1, source_target_pairs={{0,128},{128,256},{256,384},{384,0},{1,129},{129,257},{257,385},{3... | collective-permute-start | bytes 196616 | tf_op jit(solution)/shard_map/ppermute | solution.py:104
  123.1 7.4 %collective-permute-start.2 = (bf16[256,128]{1,0:T(8,128)(2,1)S(1)}, bf16[256,128]{1,0:T(8,128)(2,1)S(1)}, u32[]{:S(2)}, u32[]{:S(2)}) collective-permute-start(bf16[256,128]{1,0:T(8,128)(2,1)S(1)} %gather_fusion), channel_id=1, source_target_pairs={{0,384},{128,0},{256,128},{384,256},{1,385},{129,1},{257,129},{385... | collective-permute-start | bytes 196616 | tf_op jit(solution)/shard_map/ppermute | solution.py:106
Sparse Core Ops, SparseCore 0:
  10.8 29.8 reduce-scatter.1
